TPU v7x, 256 devices: a whole 4x4x8 slice. The times are simulated.
256 devices in a mesh: grp: 8 (over x, core), dev: 32 (over z, y).
Axes of the slice: x: 4, y: 4, z: 8, core: 2. Of those that a mesh axis runs over, the one named last changes fastest.
Arguments:
- references: bfloat16 [192, 2048], P('dev'), may hold values from -4 to 4
- particles: bfloat16 [2048, 65536], P(None, ('grp', 'dev')), may hold values from -1300 to 1300
- defocus_bin: int32 [65536], P(('grp', 'dev')), may hold values from 0 to 63
- contrast_table: float32 [64, 32], replicated, may hold values from 0.1 to 1
- noise_power: float32 [32], replicated, may hold values from 300 to 3000
- class_prior: float32 [192], replicated, may hold values from -3 to 3
Outputs:
- new_references: float32 [192, 2048], P('dev')
- occupancy: float32 [192], P('dev')
All inputs are finite; a program needn't handle non-finite values.
Results may differ from a plain program's by a relative error of at most 0.0015.
Values may be sent and summed in bfloat16 or wider, within the bound.
No kernel may reach another device: no remote copies, remote signals or barrier semaphores. Data moves between devices by JAX's collectives and lax.ppermute only.
A program may use at most 64 MiB of HBM per device.

v0:
```python
import math
import jax
import jax.numpy as jnp
from jax import lax
from jax.sharding import PartitionSpec as P

Q = 32
M = 32
R = 128
CLS_DEV = 6


def angle_tables(cycle_freqs, count_turns):
    freq_index = jnp.arange(cycle_freqs, dtype=jnp.int32)
    turn_index = jnp.arange(count_turns, dtype=jnp.int32)
    wrapped = freq_index[:, None] * turn_index[None, :] % count_turns
    phases = 2.0 * math.pi / count_turns * wrapped.astype(jnp.float32)
    factor = jnp.where(freq_index == 0, 1.0, 2.0).astype(jnp.float32)[:, None]
    cosine = jnp.cos(phases)
    sine_part = jnp.sin(phases)
    score_table = jnp.stack([factor * cosine, factor * sine_part], 0).astype(jnp.bfloat16)
    turn_table = jnp.stack([cosine, sine_part], 0).astype(jnp.bfloat16)
    return (score_table, turn_table)


def particle_terms(particles, defocus_bin, contrast_table, noise_power):
    columns = particles.shape[1]
    cycle_count = contrast_table.shape[1]
    freq_count = particles.shape[0] // (2 * cycle_count)
    onehot = (
        defocus_bin[None, :] == jnp.arange(contrast_table.shape[0], dtype=jnp.int32)[:, None]
    ).astype(jnp.float32)
    contrast = jnp.dot(contrast_table.T, onehot, precision=lax.Precision.HIGHEST)
    scaled = contrast / noise_power[:, None]
    power_term = contrast * scaled
    weighted = (
        particles.astype(jnp.float32).reshape(freq_count, 2, cycle_count, columns)
        * scaled[None, None]
    ).astype(jnp.bfloat16)
    return (weighted.reshape(freq_count, 2 * cycle_count, columns), power_term)


def class_rows(class_block):
    classes = class_block.shape[0]
    class_grid = class_block.reshape(classes, M, 2, Q)
    real_part = class_grid[:, :, 0, :]
    imag_part = class_grid[:, :, 1, :]
    rows_real = jnp.concatenate([real_part, imag_part], -1)
    rows_imag = jnp.concatenate([-imag_part, real_part], -1)
    stacked = jnp.stack([rows_real, rows_imag], 0)
    factor = jnp.where(jnp.arange(M) == 0, 1.0, 2.0).astype(jnp.float32)
    squares = class_grid.astype(jnp.float32) ** 2
    cycle_power = jnp.sum(jnp.sum(squares, axis=2) * factor[None, :, None], axis=1)
    return (stacked, cycle_power)


def block_rows(total_rows):
    return CLS_DEV * math.gcd(total_rows // CLS_DEV, 4)


def local(references, particles, defocus_bin, contrast_table, noise_power, class_prior):
    weighted, power_term = particle_terms(particles, defocus_bin, contrast_table, noise_power)
    score_table, turn_table = angle_tables(M, R)
    columns = particles.shape[1]
    classes_total = CLS_DEV * lax.axis_size("dev")

    def block_scores(class_block, first_row):
        stacked, cycle_power = class_rows(class_block)
        prior_part = lax.dynamic_slice_in_dim(class_prior, first_row, class_block.shape[0], 0)
        crossed = jnp.einsum(
            "pkmc,mcb->pmkb", stacked, weighted, preferred_element_type=jnp.float32
        ).astype(jnp.bfloat16)
        scores = jnp.einsum(
            "pmkb,pmr->krb", crossed, score_table, preferred_element_type=jnp.float32
        )
        penalty = jnp.dot(cycle_power, power_term, precision=lax.Precision.HIGHEST)
        return scores - 0.5 * penalty[:, None, :] + prior_part[:, None, None]

    initial = (jnp.full((columns,), -1e30, jnp.float32), jnp.zeros((columns,), jnp.float32))
    empty_sums = (
        jnp.zeros((classes_total, 2 * M * Q), jnp.float32),
        jnp.zeros((classes_total, Q), jnp.float32),
        jnp.zeros((classes_total,), jnp.float32),
    )
    gathered = lax.all_gather(references, "dev", axis=0, tiled=True)
    height = block_rows(gathered.shape[0])
    block_count = gathered.shape[0] // height
    blocks = gathered.reshape(block_count, height, gathered.shape[1])

    def one_block(current, block_item):
        class_block, offset = block_item
        scores = block_scores(class_block, offset * height)
        block_max = jnp.max(scores, axis=(0, 1))
        new_max = jnp.maximum(current[0], block_max)
        block_total = jnp.sum(jnp.exp(scores - new_max[None, None, :]), axis=(0, 1))
        return ((new_max, current[1] * jnp.exp(current[0] - new_max) + block_total), None)

    result, unused = lax.scan(
        one_block, initial, (blocks, jnp.arange(block_count, dtype=jnp.int32))
    )
    log_norm = result[0] + jnp.log(result[1])
    add_height = block_rows(gathered.shape[0])
    block_count = gathered.shape[0] // add_height
    blocks = gathered.reshape(block_count, add_height, gathered.shape[1])

    def one_block(current, block_item):
        class_block, offset = block_item
        row_start = offset * add_height
        scores = block_scores(class_block, row_start)
        responsibility = jnp.exp(scores - log_norm[None, None, :]).astype(jnp.bfloat16)
        spectra = jnp.einsum(
            "krb,pmr->pmkb", responsibility, turn_table, preferred_element_type=jnp.float32
        ).astype(jnp.bfloat16)
        products = jnp.einsum(
            "pmkb,mcb->kpmc", spectra, weighted, preferred_element_type=jnp.float32
        )
        real_sum = products[:, 0, :, :Q] + products[:, 1, :, Q:]
        imag_sum = products[:, 0, :, Q:] - products[:, 1, :, :Q]
        numerator = jnp.stack([real_sum, imag_sum], 2).reshape(add_height, 2 * M * Q)
        class_weight = jnp.sum(responsibility.astype(jnp.float32), axis=1)
        cycle_sum = jnp.dot(class_weight, power_term.T, precision=lax.Precision.HIGHEST)
        class_mass = jnp.sum(class_weight, axis=1)
        updated = (
            lax.dynamic_update_slice_in_dim(current[0], numerator, row_start, 0),
            lax.dynamic_update_slice_in_dim(current[1], cycle_sum, row_start, 0),
            lax.dynamic_update_slice_in_dim(current[2], class_mass, row_start, 0),
        )
        return (updated, None)

    result, unused = lax.scan(
        one_block, empty_sums, (blocks, jnp.arange(block_count, dtype=jnp.int32))
    )
    numer_all, cycles_all, mass_all = result
    width = numer_all.shape[1]
    packed = jnp.concatenate(
        [numer_all, cycles_all, mass_all[:, None], jnp.zeros((classes_total, 95), jnp.float32)], 1
    )
    packed = packed.reshape(lax.axis_size("dev"), CLS_DEV, packed.shape[1])
    own = lax.psum_scatter(packed, "dev", scatter_dimension=0, tiled=False)
    own = lax.psum(own, "grp")
    numerator = own[:, :width]
    cycle_sum = own[:, width : width + Q]
    class_mass = own[:, width + Q]
    new_references = (numerator.reshape(CLS_DEV, M, 2, Q) / cycle_sum[:, None, None, :]).reshape(
        CLS_DEV, 2 * M * Q
    )
    particle_total = columns * lax.axis_size("grp") * lax.axis_size("dev")
    occupancy = class_mass * (classes_total / particle_total)
    return (new_references, occupancy)


def solution(mesh):
    return jax.shard_map(
        local,
        mesh=mesh,
        in_specs=(P("dev", None), P(None, ("grp", "dev")), P(("grp", "dev")), P(), P(), P()),
        out_specs=(P("dev", None), P("dev")),
        check_vma=False,
    )
```

profile of v0, /device:TPU:8, one launch (start us, length us, event | category | flops | bytes accessed | tf_op | source)
XLA Modules:
  0.0 494.4 jit_solution(4730013904374642111)
XLA Ops:
  7.5 53.1 %all-gather = bf16[32,6,2048]{2,1,0:T(8,128)(2,1)S(1)} all-gather(bf16[1,6,2048]{2,1,0:T(8,128)(2,1)} %bitcast.182), channel_id=1, replica_groups=mesh['grp'=8,'dev'=32] {'dev'}, dimensions={0}, use_global_device_ids=true | all-gather | bytes 811008 | tf_op jit(solution)/shard_map/all_gather | solution.py:85
  63.9 87.8 %while.28 = (s32[]{:T(128)}, f32[256]{0:T(256)S(1)}, f32[256]{0:T(256)S(1)}, bf16[8,24,2048]{2,1,0:T(8,128)(2,1)}, bf16[32,64,256]{2,1,0:T(8,128)(2,1)}, /*index...) while((s32[]{:T(128)}, f32[256]{0:T(256)S(1)}, ...), condition=%wide.region_5.6_spmd.clone, body=%wide.region_0.5_spmd.clone.sunk | while | flops 159947328 | bytes 10727242 | solution.py:98
  66.7 2.5 fusion.112
  71.9 2.0 fusion.113
  77.6 2.5 fusion.112
  82.9 2.0 fusion.113
  88.6 2.5 fusion.112
  93.9 2.0 fusion.113
  99.6 2.5 fusion.112
  104.9 2.0 fusion.113
  110.6 2.5 fusion.112
  115.8 2.0 fusion.113
  121.6 2.5 fusion.112
  126.8 2.0 fusion.113
  132.5 2.5 fusion.112
  137.8 2.0 fusion.113
  143.5 2.5 fusion.112
  148.8 2.0 fusion.113
  152.0 106.6 %while.27 = (s32[]{:T(128)}, f32[192,2048]{1,0:T(8,128)S(1)}, f32[192,32]{1,0:T(8,128)S(1)}, f32[192]{0:T(256)S(1)}, bf16[8,24,2048]{2,1,0:T(8,128)(2,1)}, /*ind...) while((s32[]{:T(128)}, f32[192,2048]{1,0:T(8,128)S(1)}, ...), condition=%wide.region_11.12_spmd, body=%wide.region_6.11_spmd.sunk | while | flops 313785664 | bytes 12832803 | solution.py:130
  200.9 2.0 convolution_bitcast_fusion.3
  214.2 2.0 convolution_bitcast_fusion.3
  261.4 2.2 concatenate.25
  263.6 197.4 %reduce-scatter.4.cloned.1.call-done = f32[1,6,2176]{2,1,0:T(8,128)} async-done(((f32[32,6,2176]{2,1,0:T(8,128)}), f32[1,6,2176]{2,1,0:T(8,128)}) %reduce-scatter.4.cloned.1.call-update) | async-done | bytes 52240
  461.0 24.9 %psum.7 = f32[6,2176]{1,0:T(8,128)S(1)} all-reduce(f32[6,2176]{1,0:T(8,128)} %bitcast.181), channel_id=1, replica_groups=mesh['grp'=8,'dev'=32] {'grp'}, use_global_device_ids=true, to_apply=%region_13.14 | all-reduce | flops 13056 | bytes 104448 | tf_op jit(solution)/shard_map/psum | solution.py:140
  (354 shorter events, 150.6 us)
Async XLA Ops:
  7.2 54.6 %copy-start = (f32[64,32]{0,1:T(8,128)S(1)}, f32[64,32]{0,1:T(8,128)}, u32[]{:S(2)}) copy-start(f32[64,32]{0,1:T(8,128)} %param.13) | copy-start | bytes 24580
  7.2 55.5 %copy-start.2 = (bf16[2048,256]{1,0:T(8,128)(2,1)S(1)}, bf16[2048,256]{1,0:T(8,128)(2,1)}, u32[]{:S(2)}) copy-start(bf16[2048,256]{1,0:T(8,128)(2,1)} %param.11) | copy-start | bytes 3145732
  7.2 56.7 %copy-start.3 = (f32[192]{0:T(256)S(1)}, f32[192]{0:T(256)}, u32[]{:S(2)}) copy-start(f32[192]{0:T(256)} %param.15) | copy-start | bytes 2308
  7.2 453.8 %reduce-scatter.4.cloned.1.call-start = ((), (), s32[]{:S(2)}) async-start(), calls=%async_computation.1 | async-start | bytes 2297856
  258.5 1.2 copy-start.1
Sparse Core Ops, SparseCore 0:
  263.7 197.2 reduce-scatter.3
where the time goes:
time: 497 us; the launch traced here: 494 us
  waiting for transfers between devices  197 us (40%)
  matrix products  82.1 us (17%)
  blocking collectives  78 us (16%)
  local copies, waits for them, and re-layouts  68.5 us (14%)
  other arithmetic  42 us (8%)
  between operations  14.2 us (3%)
  loops' own time  12.1 us (2%)
    unnamed x2, waiting for transfers between devices  197 us
    all_gather x1, blocking collectives, local(): gathered = lax.all_gather(references, 'dev', axis=0, tiled=True)  53.1 us
    dot_general x16, matrix products, block_scores(): jnp.einsum('pkmc,mcb->pmkb', stacked, weighted, preferred_element_type=jn...  32.7 us
    dot_general x16, matrix products, block_scores(): jnp.einsum('pmkb,pmr->krb', crossed, score_table, preferred_element_type=...  26.3 us
    psum x1, blocking collectives, local(): own = lax.psum(own, 'grp')  24.9 us
    dynamic_slice x32, local copies, waits for them, and re-layouts, local(): lax.scan(one_block, initial, (blocks, jnp.arange(block_count, dtype=jnp.i...  23.9 us
    reduce_sum x16, other arithmetic, class_rows(): jnp.sum(squares, axis=2) * factor[None, :, None]  18.6 us
    dot_general x8, matrix products, one_block(): jnp.einsum('pmkb,mcb->kpmc', spectra, weighted, preferred_element_type=jn...  15.7 us
  transfers between devices with their start and end apart: 1, of which 1 were waited for; matrix products, arithmetic and copies ran while one was open for 0% of the time, Pallas kernels for 0%

commit v1 on v0

--- a/solution.py
+++ b/solution.py
@@ -82,7 +82,9 @@
         jnp.zeros((classes_total, Q), jnp.float32),
         jnp.zeros((classes_total,), jnp.float32),
     )
-    gathered = lax.all_gather(references, "dev", axis=0, tiled=True)
+    gathered = jnp.concatenate(
+        lax.all_to_all(jnp.stack([references] * lax.axis_size("dev")), "dev", 0, 0), axis=0
+    )
     height = block_rows(gathered.shape[0])
     block_count = gathered.shape[0] // height
     blocks = gathered.reshape(block_count, height, gathered.shape[1])

time: 497 us -> 482 us (0.970)
  blocking collectives: 78 us -> 24.9 us
  waiting for transfers between devices: 197 us -> 223 us
  starting transfers between devices: 0.04 us -> 11.9 us
    all_gather x1 -> x0, blocking collectives: 53.1 us -> none  [local(): gathered = lax.all_gather(references, 'dev', axis=0, tiled=True)]
    all_to_all x0 -> x1, waiting for transfers between devices: none -> 26.3 us  [local(): lax.all_to_all(jnp.stack([references] * lax.axis_size('dev')), 'dev', 0, 0)]
    all_to_all x0 -> x1, starting transfers between devices: none -> 11.8 us  [local(): lax.all_to_all(jnp.stack([references] * lax.axis_size('dev')), 'dev', 0, 0)]
  transfers between devices with their start and end apart: 1 -> 2, of which waited for: 1 -> 2; matrix products, arithmetic and copies ran while one was open for 0% -> 0% of each run, Pallas kernels for 0% -> 0%
where the time goes in v1:
time: 482 us; the launch traced here: 480 us
  waiting for transfers between devices  223 us (46%)
  matrix products  81.4 us (17%)
  local copies, waits for them, and re-layouts  70.5 us (15%)
  other arithmetic  42 us (9%)
  blocking collectives  24.9 us (5%)
  between operations  14.3 us (3%)
  loops' own time  12.1 us (3%)
  starting transfers between devices  11.9 us (2%)
    unnamed x2, waiting for transfers between devices  196 us
    dot_general x16, matrix products, block_scores(): jnp.einsum('pkmc,mcb->pmkb', stacked, weighted, preferred_element_type=jn...  32.7 us
    all_to_all x1, waiting for transfers between devices, local(): lax.all_to_all(jnp.stack([references] * lax.axis_size('dev')), 'dev', 0, 0)  26.3 us
    dot_general x16, matrix products, block_scores(): jnp.einsum('pmkb,pmr->krb', crossed, score_table, preferred_element_type=...  26.3 us
    psum x1, blocking collectives, local(): own = lax.psum(own, 'grp')  24.9 us
    dynamic_slice x32, local copies, waits for them, and re-layouts, local(): lax.scan(one_block, initial, (blocks, jnp.arange(block_count, dtype=jnp.i...  23.9 us
    reduce_sum x16, other arithmetic, class_rows(): jnp.sum(squares, axis=2) * factor[None, :, None]  18.6 us
    dot_general x8, matrix products, one_block(): jnp.einsum('pmkb,mcb->kpmc', spectra, weighted, preferred_element_type=jn...  15.7 us
  transfers between devices with their start and end apart: 2, of which 2 were waited for; matrix products, arithmetic and copies ran while one was open for 0% of the time, Pallas kernels for 0%

profile of v1, /device:TPU:8, one launch (start us, length us, event | category | flops | bytes accessed | tf_op | source)
XLA Modules:
  0.0 479.8 jit_solution(3250641396538998352)
XLA Ops:
  7.2 2.0 stack.22
  9.2 11.8 %all-to-all-start = ((bf16[32,6,2048]{2,1,0:T(8,128)(2,1)}), bf16[32,6,2048]{2,1,0:T(8,128)(2,1)S(1)}, u32[]{:S(2)}, u32[]{:S(2)}) async-start(bf16[32,6,2048]{2,1,0:T(8,128)(2,1)} %stack.22), calls=%async_computation | async-start | bytes 2097152 | tf_op jit(solution)/shard_map/all_to_all | solution.py:86
  22.8 26.3 %all-to-all-done = bf16[32,6,2048]{2,1,0:T(8,128)(2,1)S(1)} async-done(((bf16[32,6,2048]{2,1,0:T(8,128)(2,1)}), bf16[32,6,2048]{2,1,0:T(8,128)(2,1)S(1)}, u32[]{:S(2)}, u32[]{:S(2)}) %all-to-all-start) | async-done | bytes 786464 | tf_op jit(solution)/shard_map/all_to_all | solution.py:86
  50.3 87.8 %while.28 = (s32[]{:T(128)}, f32[256]{0:T(256)S(1)}, f32[256]{0:T(256)S(1)}, bf16[8,24,2048]{2,1,0:T(8,128)(2,1)}, bf16[32,64,256]{2,1,0:T(8,128)(2,1)}, /*index...) while((s32[]{:T(128)}, f32[256]{0:T(256)S(1)}, ...), condition=%wide.region_5.6_spmd.clone, body=%wide.region_0.5_spmd.clone.sunk | while | flops 159947328 | bytes 10727242 | solution.py:100
  53.1 2.5 fusion.112
  58.3 2.0 fusion.113
  64.1 2.5 fusion.112
  69.3 2.0 fusion.113
  75.0 2.5 fusion.112
  80.3 2.0 fusion.113
  86.0 2.5 fusion.112
  91.3 2.0 fusion.113
  97.0 2.5 fusion.112
  102.3 2.0 fusion.113
  108.0 2.5 fusion.112
  113.2 2.0 fusion.113
  119.0 2.5 fusion.112
  124.2 2.0 fusion.113
  129.9 2.5 fusion.112
  135.2 2.0 fusion.113
  138.4 106.6 %while.27 = (s32[]{:T(128)}, f32[192,2048]{1,0:T(8,128)S(1)}, f32[192,32]{1,0:T(8,128)S(1)}, f32[192]{0:T(256)S(1)}, bf16[8,24,2048]{2,1,0:T(8,128)(2,1)}, /*ind...) while((s32[]{:T(128)}, f32[192,2048]{1,0:T(8,128)S(1)}, ...), condition=%wide.region_11.12_spmd, body=%wide.region_6.11_spmd.sunk | while | flops 313785664 | bytes 12832803 | solution.py:132
  247.8 2.2 concatenate.25
  250.0 196.4 %reduce-scatter.4.cloned.1.call-done = f32[1,6,2176]{2,1,0:T(8,128)} async-done(((f32[32,6,2176]{2,1,0:T(8,128)}), f32[1,6,2176]{2,1,0:T(8,128)}) %reduce-scatter.4.cloned.1.call-update) | async-done | bytes 52240
  446.5 24.9 %psum.7 = f32[6,2176]{1,0:T(8,128)S(1)} all-reduce(f32[6,2176]{1,0:T(8,128)} %bitcast.180), channel_id=1, replica_groups=mesh['grp'=8,'dev'=32] {'grp'}, use_global_device_ids=true, to_apply=%region_13.14 | all-reduce | flops 13056 | bytes 104448 | tf_op jit(solution)/shard_map/psum | solution.py:142
  (360 shorter events, 153.8 us)
Async XLA Ops:
  7.2 14.2 %copy-start = (f32[64,32]{0,1:T(8,128)S(1)}, f32[64,32]{0,1:T(8,128)}, u32[]{:S(2)}) copy-start(f32[64,32]{0,1:T(8,128)} %param.13) | copy-start | bytes 24580
  7.2 14.2 %copy-start.3 = (s32[256]{0:T(256)S(1)}, s32[256]{0:T(256)}, u32[]{:S(2)}) copy-start(s32[256]{0:T(256)} %param.12) | copy-start | bytes 3076
  7.2 14.2 %copy-start.5 = (f32[32]{0:T(128)S(1)}, f32[32]{0:T(128)}, u32[]{:S(2)}) copy-start(f32[32]{0:T(128)} %param.14) | copy-start | bytes 388
  7.2 14.3 %copy-start.2 = (bf16[2048,256]{1,0:T(8,128)(2,1)S(1)}, bf16[2048,256]{1,0:T(8,128)(2,1)}, u32[]{:S(2)}) copy-start(bf16[2048,256]{1,0:T(8,128)(2,1)} %param.11) | copy-start | bytes 3145732
  9.2 41.1 %copy-start.4 = (f32[192]{0:T(256)S(1)}, f32[192]{0:T(256)}, u32[]{:S(2)}) copy-start(f32[192]{0:T(256)} %param.15) | copy-start | bytes 2308
  9.2 39.9 %all-to-all-start = ((bf16[32,6,2048]{2,1,0:T(8,128)(2,1)}), bf16[32,6,2048]{2,1,0:T(8,128)(2,1)S(1)}, u32[]{:S(2)}, u32[]{:S(2)}) async-start(bf16[32,6,2048]{2,1,0:T(8,128)(2,1)} %stack.22), calls=%async_computation | async-start | bytes 2097152 | tf_op jit(solution)/shard_map/all_to_all | solution.py:86
  21.1 425.4 %reduce-scatter.4.cloned.1.call-start = ((), (), s32[]{:S(2)}) async-start(), calls=%async_computation.2 | async-start | bytes 2297856
  244.9 1.2 copy-start.1
Sparse Core Ops, SparseCore 0:
  250.1 196.2 reduce-scatter.3
